TPU v7x, 512 devices: a whole 4x4x16 slice. The times are simulated.
512 devices in a mesh: pos: 64 (over z, y), mode: 8 (over x, core).
Axes of the slice: x: 4, y: 4, z: 16, core: 2. Of those that a mesh axis runs over, the one named last changes fastest.
Arguments:
- object_field: float32 [2, 8192, 512], P(None, 'pos'), may hold values from -6 to 6
- probe: float32 [2, 8, 256, 256], P(None, 'mode'), may hold values from -3 to 3
- measured: float32 [192, 256, 256], P('pos'), may hold values from 0 to 16
- row_offsets: int32 [192], P('pos'), may hold values from 0 to 127
- col_offsets: int32 [192], P('pos'), may hold values from 0 to 256
- tile_counts: int32 [64], P('pos'), may hold values from 1 to 3, 96 in all
Outputs:
- updated_object: float32 [2, 8192, 512], P(None, ('pos', 'mode'))
Inputs may be any that keep to these rules, and one draw needn't show every extreme that they name: Slots 0 to tile_counts[t] - 1 of tile t hold scan positions, the others are empty; the counts sum to 96 and the largest equals 3.
All inputs are finite; a program needn't handle non-finite values. No bound on the sum of `tile_counts` on one device may be relied on, other than what follows from the above.
Results may differ from a plain program's by a relative error of at most 0.0016.
Values sent between devices are 32-bit elements; how exact they have to be, the bound alone decides.
No kernel may reach another device: no remote copies, remote signals or barrier semaphores. Data moves between devices by JAX's collectives and lax.ppermute only.
A program may use at most 64 MiB of HBM per device.

v0:
```python
import math
import jax
import jax.numpy as jnp
from jax import lax
from jax.sharding import PartitionSpec as P


def extended_2(array, sides, width):
    for axis, dim in sides:
        size, length = (lax.axis_size(axis), array.shape[dim])
        up = [(i, (i + 1) % size) for i in range(size - 1)]
        down = [(j, i) for i, j in up]
        last = lax.slice_in_dim(array, length - width, length, axis=dim)
        first = lax.slice_in_dim(array, 0, width, axis=dim)
        before = lax.ppermute(last, axis, up)
        after = lax.ppermute(first, axis, down)
        array = jnp.concatenate([before, array, after], axis=dim)
    return array


def dft_tables(pattern):
    counter = jnp.arange(pattern, dtype=jnp.int32)
    phases = counter[:, None] * counter[None, :] % pattern
    angles = phases.astype(jnp.float32) * (2.0 * math.pi / pattern)
    factor = 1.0 / math.sqrt(pattern)
    return (
        (jnp.cos(angles) * factor).astype(jnp.bfloat16),
        (-jnp.sin(angles) * factor).astype(jnp.bfloat16),
    )


def left_product(table, stacked):
    return jnp.einsum("ua,kab->kub", table, stacked, preferred_element_type=jnp.float32)


def right_product(stacked, table):
    return jnp.einsum("kub,bv->kuv", stacked, table, preferred_element_type=jnp.float32)


def local(object_field, probe, measured, row_offsets, col_offsets, tile_counts):
    rows_tile = object_field.shape[1]
    columns = object_field.shape[2]
    pattern = probe.shape[2]
    slot_count = measured.shape[0]
    mode_count = lax.axis_size("mode")
    my_mode = lax.axis_index("mode")
    share_rows = rows_tile // mode_count
    real_table, imag_table = dft_tables(pattern)
    anchor = jnp.zeros((), jnp.int32)
    extended = extended_2(object_field, (("pos", 1),), rows_tile)
    probe_re = probe[0]
    probe_im = probe[1]
    top_rows = rows_tile + row_offsets - pattern // 2

    def forward(position):
        window = lax.dynamic_slice(
            extended, (anchor, top_rows[position], col_offsets[position]), (2, pattern, pattern)
        )
        exit_re = (probe_re * window[0] - probe_im * window[1]).astype(jnp.bfloat16)
        exit_im = (probe_re * window[1] + probe_im * window[0]).astype(jnp.bfloat16)
        half_re = (left_product(real_table, exit_re) - left_product(imag_table, exit_im)).astype(
            jnp.bfloat16
        )
        half_im = (left_product(real_table, exit_im) + left_product(imag_table, exit_re)).astype(
            jnp.bfloat16
        )
        wave_re = right_product(half_re, real_table) - right_product(half_im, imag_table)
        wave_im = right_product(half_re, imag_table) + right_product(half_im, real_table)
        return (exit_re, exit_im, wave_re, wave_im)

    exit_re, exit_im, wave_re, wave_im = lax.map(forward, jnp.arange(slot_count, dtype=jnp.int32))
    power_sum = jnp.sum(wave_re * wave_re + wave_im * wave_im, axis=1)
    model_power = lax.psum(power_sum, "mode")
    scaling = jnp.sqrt(measured) / jnp.maximum(jnp.sqrt(model_power), 1.0)
    probe_power = jnp.sum(probe_re * probe_re + probe_im * probe_im, axis=0)
    live_count = tile_counts[0]

    def backward(position, buffer):
        fixed_re = (scaling[position] * wave_re[position]).astype(jnp.bfloat16)
        fixed_im = (scaling[position] * wave_im[position]).astype(jnp.bfloat16)
        back_re = (left_product(real_table, fixed_re) + left_product(imag_table, fixed_im)).astype(
            jnp.bfloat16
        )
        back_im = (left_product(real_table, fixed_im) - left_product(imag_table, fixed_re)).astype(
            jnp.bfloat16
        )
        delta_re = (
            right_product(back_re, real_table)
            + right_product(back_im, imag_table)
            - exit_re[position].astype(jnp.float32)
        )
        delta_im = (
            right_product(back_im, real_table)
            - right_product(back_re, imag_table)
            - exit_im[position].astype(jnp.float32)
        )
        numer_re = jnp.sum(probe_re * delta_re + probe_im * delta_im, axis=0)
        numer_im = jnp.sum(probe_re * delta_im - probe_im * delta_re, axis=0)
        contrib = jnp.stack([numer_re, numer_im, probe_power])
        contrib = jnp.where(position < live_count, contrib, jnp.zeros_like(contrib))
        corner = (anchor, top_rows[position], col_offsets[position])
        current = lax.dynamic_slice(buffer, corner, (3, pattern, pattern))
        return lax.dynamic_update_slice(buffer, current + contrib, corner)

    buffer = lax.fori_loop(
        0, slot_count, backward, jnp.zeros((3, 3 * rows_tile, columns), jnp.float32)
    )
    outside = jnp.concatenate([buffer[:, :rows_tile], buffer[:, 2 * rows_tile :]], axis=1)
    framed_sum = extended_2(outside, (("pos", 1),), rows_tile)
    tile_sum = (
        buffer[:, rows_tile : 2 * rows_tile]
        + framed_sum[:, :rows_tile]
        + framed_sum[:, 3 * rows_tile :]
    )
    update_sum = lax.psum_scatter(tile_sum, "mode", scatter_dimension=1, tiled=True)
    own_rows = lax.dynamic_slice_in_dim(object_field, my_mode * share_rows, share_rows, 1)
    return own_rows + update_sum[:2] / (update_sum[2] + 1.0)


def solution(mesh):
    in_specs = (
        P(None, "pos", None),
        P(None, "mode", None, None),
        P("pos", None, None),
        P("pos"),
        P("pos"),
        P("pos"),
    )
    out_specs = P(None, ("pos", "mode"), None)
    return jax.shard_map(local, mesh=mesh, in_specs=in_specs, out_specs=out_specs, check_vma=False)
```

profile of v0, /device:TPU:8, one launch (start us, length us, event | category | flops | bytes accessed | tf_op | source)
XLA Modules:
  0.0 350.2 jit_solution(2317298614045170838)
XLA Ops:
  6.5 3.6 %collective-permute-start = (f32[2,128,512]{2,1,0:T(8,128)}, f32[2,128,512]{2,1,0:T(8,128)S(1)}, u32[]{:S(2)}, u32[]{:S(2)}) collective-permute-start(f32[2,128,512]{2,1,0:T(8,128)} %param.10), channel_id=1, source_target_pairs={{0,8},{8,16},{16,24},{24,32},{32,40},{40,48},{48,56},{56,64},{64,7... | collective-permute-start | bytes 1572872 | tf_op jit(solution)/shard_map/ppermute | solution.py:15
  10.2 5.6 %collective-permute-start.1 = (f32[2,128,512]{2,1,0:T(8,128)}, f32[2,128,512]{2,1,0:T(8,128)S(1)}, u32[]{:S(2)}, u32[]{:S(2)}) collective-permute-start(f32[2,128,512]{2,1,0:T(8,128)} %param.10), channel_id=1, source_target_pairs={{8,0},{16,8},{24,16},{32,24},{40,32},{48,40},{56,48},{64,56},{72,6... | collective-permute-start | bytes 1572872 | tf_op jit(solution)/shard_map/ppermute | solution.py:16
  15.8 1.9 add_bitcast_fusion
  17.7 4.8 %collective-permute-done = f32[2,128,512]{2,1,0:T(8,128)S(1)} collective-permute-done((f32[2,128,512]{2,1,0:T(8,128)}, f32[2,128,512]{2,1,0:T(8,128)S(1)}, u32[]{:S(2)}, u32[]{:S(2)}) %collective-permute-start) | collective-permute-done | bytes 524320 | tf_op jit(solution)/shard_map/ppermute | solution.py:15
  22.4 3.2 collective-permute-done.1
  25.6 1.2 pad_maximum_fusion
  26.8 60.4 %while.33 = (s32[]{:T(128)}, bf16[3,1,256,256]{3,2,1,0:T(8,128)(2,1)}, bf16[3,1,256,256]{3,2,1,0:T(8,128)(2,1)}, f32[3,1,256,256]{3,2,1,0:T(8,128)}, f32[3,1,256...) while((s32[]{:T(128)}, ...), condition=%wide.region_1.2_spmd.clone.clone, body=%wide.region_0.1_spmd.clone.clone.sunk | while | flops 278003712 | bytes 5506879 | solution.py:71
  34.4 2.0 bitcast_dynamic-update-slice_fusion.3
  37.5 1.1 fusion.198
  39.8 1.1 fusion.195
  42.1 1.9 fusion.201
  45.1 1.9 fusion.199
  54.5 1.9 bitcast_dynamic-update-slice_fusion.3
  57.6 1.1 fusion.198
  62.2 1.9 fusion.201
  65.2 1.9 fusion.199
  74.7 2.0 bitcast_dynamic-update-slice_fusion.3
  82.3 1.9 fusion.201
  85.3 1.9 fusion.199
  87.2 2.5 fusion.136
  89.9 83.1 %all-reduce.2.cloned.1.call-done = f32[3,256,256]{2,1,0:T(8,128)} async-done(((f32[3,256,256]{2,1,0:T(8,128)}), f32[3,256,256]{2,1,0:T(8,128)}) %all-reduce.2.cloned.1.call-update) | async-done | bytes 786448 | tf_op jit(solution)/shard_map/psum | solution.py:73
  173.0 2.5 maximum_divide_fusion
  175.8 99.1 %while.34 = (s32[]{:T(128)}, f32[3,384,512]{2,1,0:T(8,128)S(1)}, s32[3]{0:T(128)S(1)}, s32[3]{0:T(128)S(1)}, s32[]{:T(128)}, /*index=5*/f32[1,256,256]{2,1,0:T(8...) while((s32[]{:T(128)}, f32[3,384,512]{2,1,0:T(8,128)S(1)}, ...), condition=%wide.region_4.5_spmd.clone.clone, body=%wide.region_3.4_spmd.clone.clone.sunk | while | flops 279183360 | bytes 10223899 | solution.py:105
  175.8 1.2 fusion.210
  178.1 1.1 fusion.212
  182.7 2.1 fusion.216
  185.9 3.1 fusion.218
  195.1 1.3 fusion.219
  196.4 13.6 %dynamic_update_slice.42 = f32[3,384,512]{2,1,0:T(8,128)S(1)} dynamic-update-slice(f32[3,384,512]{2,1,0:T(8,128)S(1)} %get-tuple-element.786, f32[3,256,256]{2,1,0:T(8,128)S(1)} %fusion.219, s32[]{:T(128)} %constant.88.clone.1..sunk.1, s32[]{:T(128)S(6)} %select_n.210, s32[]{:T(128)S(6)} %select_n.211) | dynamic-update-slice | bytes 1572868 | tf_op jit(solution)/shard_map/while/body/eval_jaxpr/dynamic_update_slice | solution.py:103
  210.0 1.2 fusion.210
  215.8 1.1 fusion.215
  216.9 2.1 fusion.216
  220.1 3.1 fusion.218
  229.3 1.3 fusion.219
  230.7 11.0 %dynamic_update_slice.42 = f32[3,384,512]{2,1,0:T(8,128)S(1)} dynamic-update-slice(f32[3,384,512]{2,1,0:T(8,128)S(1)} %get-tuple-element.786, f32[3,256,256]{2,1,0:T(8,128)S(1)} %fusion.219, s32[]{:T(128)} %constant.88.clone.1..sunk.1, s32[]{:T(128)S(6)} %select_n.210, s32[]{:T(128)S(6)} %select_n.211) | dynamic-update-slice | bytes 1572868 | tf_op jit(solution)/shard_map/while/body/eval_jaxpr/dynamic_update_slice | solution.py:103
  241.7 1.2 fusion.210
  244.0 1.1 fusion.212
  248.6 2.1 fusion.216
  251.8 3.1 fusion.218
  261.0 1.3 fusion.219
  262.4 12.6 %dynamic_update_slice.42 = f32[3,384,512]{2,1,0:T(8,128)S(1)} dynamic-update-slice(f32[3,384,512]{2,1,0:T(8,128)S(1)} %get-tuple-element.786, f32[3,256,256]{2,1,0:T(8,128)S(1)} %fusion.219, s32[]{:T(128)} %constant.88.clone.1..sunk.1, s32[]{:T(128)S(6)} %select_n.210, s32[]{:T(128)S(6)} %select_n.211) | dynamic-update-slice | bytes 1572868 | tf_op jit(solution)/shard_map/while/body/eval_jaxpr/dynamic_update_slice | solution.py:103
  275.1 1.9 collective-permute-start.2
  277.1 4.0 %collective-permute-start.3 = (f32[3,128,512]{2,1,0:T(8,128)S(1)}, f32[3,128,512]{2,1,0:T(8,128)S(1)}, u32[]{:S(2)}, u32[]{:S(2)}) collective-permute-start(f32[3,128,512]{2,1,0:T(8,128)S(1)} %get-tuple-element.551), channel_id=1, source_target_pairs={{8,0},{16,8},{24,16},{32,24},{40,32},{48,40},{56,48},{64,56},{72,6... | collective-permute-start | bytes 2359304 | tf_op jit(solution)/shard_map/ppermute | solution.py:16
  281.0 13.6 %collective-permute-done.2 = f32[3,128,512]{2,1,0:T(8,128)S(1)} collective-permute-done((f32[3,128,512]{2,1,0:T(8,128)S(1)}, f32[3,128,512]{2,1,0:T(8,128)S(1)}, u32[]{:S(2)}, u32[]{:S(2)}) %collective-permute-start.2) | collective-permute-done | bytes 786464 | tf_op jit(solution)/shard_map/ppermute | solution.py:15
  294.6 3.6 %collective-permute-done.3 = f32[3,128,512]{2,1,0:T(8,128)S(1)} collective-permute-done((f32[3,128,512]{2,1,0:T(8,128)S(1)}, f32[3,128,512]{2,1,0:T(8,128)S(1)}, u32[]{:S(2)}, u32[]{:S(2)}) %collective-permute-start.3) | collective-permute-done | bytes 786464 | tf_op jit(solution)/shard_map/ppermute | solution.py:16
  298.2 1.2 add_add_fusion
  299.4 41.7 %reduce-scatter.2.cloned.1.call-done = f32[3,16,512]{2,1,0:T(8,128)} async-done(((f32[3,128,512]{2,1,0:T(8,128)}), f32[3,16,512]{2,1,0:T(8,128)}) %reduce-scatter.2.cloned.1.call-update) | async-done | bytes 98320 | tf_op jit(solution)/shard_map/reduce_scatter | solution.py:115
  341.8 1.5 fusion.137
  (63 shorter events, 45.1 us)
Async XLA Ops:
  6.5 20.3 %copy-start.1 = (s32[3]{0:T(128)S(1)}, s32[3]{0:T(128)}, u32[]{:S(2)}) copy-start(s32[3]{0:T(128)} %param.13) | copy-start | bytes 40
  6.5 20.3 %copy-start.2 = (s32[3]{0:T(128)S(1)}, s32[3]{0:T(128)}, u32[]{:S(2)}) copy-start(s32[3]{0:T(128)} %param.14) | copy-start | bytes 40
  6.5 166.5 %all-reduce.2.cloned.1.call-start = ((), (), s32[]{:S(2)}) async-start(), calls=%async_computation.1 | async-start | bytes 1572864 | tf_op jit(solution)/shard_map/psum | solution.py:73
  6.5 15.9 %collective-permute-start = (f32[2,128,512]{2,1,0:T(8,128)}, f32[2,128,512]{2,1,0:T(8,128)S(1)}, u32[]{:S(2)}, u32[]{:S(2)}) collective-permute-start(f32[2,128,512]{2,1,0:T(8,128)} %param.10), channel_id=1, source_target_pairs={{0,8},{8,16},{16,24},{24,32},{32,40},{40,48},{48,56},{56,64},{64,7... | collective-permute-start | bytes 1572872 | tf_op jit(solution)/shard_map/ppermute | solution.py:15
  10.2 15.5 %collective-permute-start.1 = (f32[2,128,512]{2,1,0:T(8,128)}, f32[2,128,512]{2,1,0:T(8,128)S(1)}, u32[]{:S(2)}, u32[]{:S(2)}) collective-permute-start(f32[2,128,512]{2,1,0:T(8,128)} %param.10), channel_id=1, source_target_pairs={{8,0},{16,8},{24,16},{32,24},{40,32},{48,40},{56,48},{64,56},{72,6... | collective-permute-start | bytes 1572872 | tf_op jit(solution)/shard_map/ppermute | solution.py:16
  87.2 85.8 %copy-start = (f32[3,256,256]{2,1,0:T(8,128)S(1)}, f32[3,256,256]{2,1,0:T(8,128)}, u32[]{:S(2)}) copy-start(f32[3,256,256]{2,1,0:T(8,128)} %param.12) | copy-start | bytes 2359300
  89.7 251.4 %reduce-scatter.2.cloned.1.call-start = ((), (), s32[]{:S(2)}) async-start(), calls=%async_computation.2 | async-start | bytes 884736 | tf_op jit(solution)/shard_map/reduce_scatter | solution.py:115
  275.1 19.5 %collective-permute-start.2 = (f32[3,128,512]{2,1,0:T(8,128)S(1)}, f32[3,128,512]{2,1,0:T(8,128)S(1)}, u32[]{:S(2)}, u32[]{:S(2)}) collective-permute-start(f32[3,128,512]{2,1,0:T(8,128)S(1)} %get-tuple-element.550), channel_id=1, source_target_pairs={{0,8},{8,16},{16,24},{24,32},{32,40},{40,48},{48,56},{56,64},{64,7... | collective-permute-start | bytes 2359304 | tf_op jit(solution)/shard_map/ppermute | solution.py:15
  277.1 21.1 %collective-permute-start.3 = (f32[3,128,512]{2,1,0:T(8,128)S(1)}, f32[3,128,512]{2,1,0:T(8,128)S(1)}, u32[]{:S(2)}, u32[]{:S(2)}) collective-permute-start(f32[3,128,512]{2,1,0:T(8,128)S(1)} %get-tuple-element.551), channel_id=1, source_target_pairs={{8,0},{16,8},{24,16},{32,24},{40,32},{48,40},{56,48},{64,56},{72,6... | collective-permute-start | bytes 2359304 | tf_op jit(solution)/shard_map/ppermute | solution.py:16
Sparse Core Ops, SparseCore 0:
  89.8 83.1 all-reduce.1
  299.5 41.5 reduce-scatter.1
where the time goes:
time: 351 us; the launch traced here: 350 us
  waiting for transfers between devices  150 us (43%)
  matrix products  67.6 us (19%)
  local copies, waits for them, and re-layouts  47.3 us (13%)
  loops' own time  31.8 us (9%)
  other arithmetic  24.8 us (7%)
  starting transfers between devices  15.3 us (4%)
  between operations  13.5 us (4%)
    psum x1, waiting for transfers between devices, local(): model_power = lax.psum(power_sum, 'mode')  83.1 us
    reduce_scatter x1, waiting for transfers between devices, local(): lax.psum_scatter(tile_sum, 'mode', scatter_dimension=1, tiled=True)  41.7 us
    dot_general x24, matrix products, right_product(): jnp.einsum('kub,bv->kuv', stacked, table, preferred_element_type=jnp.floa...  40.3 us
    dynamic_update_slice x3, local copies, waits for them, and re-layouts, backward(): return lax.dynamic_update_slice(buffer, current + contrib, corner)  37.2 us
    dot_general x24, matrix products, left_product(): jnp.einsum('ua,kab->kub', table, stacked, preferred_element_type=jnp.floa...  27.3 us
    ppermute x2, waiting for transfers between devices, extended_2(): before = lax.ppermute(last, axis, up)  18.4 us
    another operation x1, loops' own time, local(): lax.map(forward, jnp.arange(slot_count, dtype=jnp.int32))  17.2 us
    another operation x1, loops' own time, local(): lax.fori_loop(0, slot_count, backward, jnp.zeros((3, 3 * rows_tile, colum...  14.6 us
  transfers between devices with their start and end apart: 6, of which 6 were waited for; matrix products, arithmetic and copies ran while one was open for 1% of the time, Pallas kernels for 0%

commit v1 on v0

--- a/solution.py
+++ b/solution.py
@@ -70,7 +70,7 @@
 
     exit_re, exit_im, wave_re, wave_im = lax.map(forward, jnp.arange(slot_count, dtype=jnp.int32))
     power_sum = jnp.sum(wave_re * wave_re + wave_im * wave_im, axis=1)
-    model_power = lax.psum(power_sum, "mode")
+    model_power = jnp.sum(lax.all_gather(power_sum, "mode"), axis=0)
     scaling = jnp.sqrt(measured) / jnp.maximum(jnp.sqrt(model_power), 1.0)
     probe_power = jnp.sum(probe_re * probe_re + probe_im * probe_im, axis=0)
     live_count = tile_counts[0]

time: 351 us -> 323 us (0.920)
  waiting for transfers between devices: 150 us -> 122 us
    psum x1 -> x0, waiting for transfers between devices: 83.1 us -> none  [local(): model_power = lax.psum(power_sum, 'mode')]
    all_gather x0 -> x1, waiting for transfers between devices: none -> 54.6 us  [local(): model_power = jnp.sum(lax.all_gather(power_sum, 'mode'), axis=0)]
where the time goes in v1:
time: 323 us; the launch traced here: 322 us
  waiting for transfers between devices  122 us (38%)
  matrix products  67.6 us (21%)
  local copies, waits for them, and re-layouts  46.7 us (14%)
  loops' own time  29.6 us (9%)
  other arithmetic  27 us (8%)
  starting transfers between devices  15.3 us (5%)
  between operations  13.5 us (4%)
    all_gather x1, waiting for transfers between devices, local(): model_power = jnp.sum(lax.all_gather(power_sum, 'mode'), axis=0)  54.6 us
    dot_general x24, matrix products, right_product(): jnp.einsum('kub,bv->kuv', stacked, table, preferred_element_type=jnp.floa...  40.3 us
    reduce_scatter x1, waiting for transfers between devices, local(): lax.psum_scatter(tile_sum, 'mode', scatter_dimension=1, tiled=True)  39.9 us
    dynamic_update_slice x3, local copies, waits for them, and re-layouts, backward(): return lax.dynamic_update_slice(buffer, current + contrib, corner)  37.2 us
    dot_general x24, matrix products, left_product(): jnp.einsum('ua,kab->kub', table, stacked, preferred_element_type=jnp.floa...  27.3 us
    ppermute x2, waiting for transfers between devices, extended_2(): before = lax.ppermute(last, axis, up)  20.5 us
    another operation x1, loops' own time, local(): lax.map(forward, jnp.arange(slot_count, dtype=jnp.int32))  17.3 us
    another operation x1, loops' own time, local(): lax.fori_loop(0, slot_count, backward, jnp.zeros((3, 3 * rows_tile, colum...  12.3 us
  transfers between devices with their start and end apart: 6, of which 6 were waited for; matrix products, arithmetic and copies ran while one was open for 1% of the time, Pallas kernels for 0%

profile of v1, /device:TPU:8, one launch (start us, length us, event | category | flops | bytes accessed | tf_op | source)
XLA Modules:
  0.0 321.9 jit_solution(16533029531524323770)
XLA Ops:
  6.5 3.6 %collective-permute-start = (f32[2,128,512]{2,1,0:T(8,128)}, f32[2,128,512]{2,1,0:T(8,128)S(1)}, u32[]{:S(2)}, u32[]{:S(2)}) collective-permute-start(f32[2,128,512]{2,1,0:T(8,128)} %param.10), channel_id=1, source_target_pairs={{0,8},{8,16},{16,24},{24,32},{32,40},{40,48},{48,56},{56,64},{64,7... | collective-permute-start | bytes 1572872 | tf_op jit(solution)/shard_map/ppermute | solution.py:15
  10.2 5.6 %collective-permute-start.1 = (f32[2,128,512]{2,1,0:T(8,128)}, f32[2,128,512]{2,1,0:T(8,128)S(1)}, u32[]{:S(2)}, u32[]{:S(2)}) collective-permute-start(f32[2,128,512]{2,1,0:T(8,128)} %param.10), channel_id=1, source_target_pairs={{8,0},{16,8},{24,16},{32,24},{40,32},{48,40},{56,48},{64,56},{72,6... | collective-permute-start | bytes 1572872 | tf_op jit(solution)/shard_map/ppermute | solution.py:16
  15.8 1.9 add_bitcast_fusion
  17.7 4.8 %collective-permute-done = f32[2,128,512]{2,1,0:T(8,128)S(1)} collective-permute-done((f32[2,128,512]{2,1,0:T(8,128)}, f32[2,128,512]{2,1,0:T(8,128)S(1)}, u32[]{:S(2)}, u32[]{:S(2)}) %collective-permute-start) | collective-permute-done | bytes 524320 | tf_op jit(solution)/shard_map/ppermute | solution.py:15
  22.4 3.2 collective-permute-done.1
  25.6 1.2 pad_maximum_fusion
  26.8 60.4 %while.33 = (s32[]{:T(128)}, bf16[3,1,256,256]{3,2,1,0:T(8,128)(2,1)}, bf16[3,1,256,256]{3,2,1,0:T(8,128)(2,1)}, f32[3,1,256,256]{3,2,1,0:T(8,128)}, f32[3,1,256...) while((s32[]{:T(128)}, ...), condition=%wide.region_1.2_spmd.clone.clone, body=%wide.region_0.1_spmd.clone.clone.sunk | while | flops 278003712 | bytes 5506879 | solution.py:71
  34.4 2.0 bitcast_dynamic-update-slice_fusion.3
  37.6 1.1 fusion.196
  39.8 1.1 fusion.193
  42.1 1.9 fusion.199
  45.2 1.9 fusion.197
  54.6 2.0 bitcast_dynamic-update-slice_fusion.3
  62.3 1.9 fusion.199
  65.3 1.9 fusion.197
  74.7 2.0 bitcast_dynamic-update-slice_fusion.3
  82.4 1.9 fusion.199
  85.4 1.9 fusion.197
  87.3 2.4 multiply_add_fusion
  90.0 54.6 %all-gather.3.cloned.1.call-done = f32[24,1,256,256]{3,2,1,0:T(8,128)} async-done(((f32[3,1,256,256]{3,2,1,0:T(8,128)}), f32[24,1,256,256]{3,2,1,0:T(8,128)}) %all-gather.3.cloned.1.call-update) | async-done | bytes 6291472 | tf_op jit(solution)/shard_map/all_gather | solution.py:73
  144.6 3.4 %bitcast_reduce_fusion = f32[3,256,256]{2,1,0:T(8,128)S(1)} fusion(f32[8,3,256,256]{3,2,1,0:T(8,128)} %bitcast.195), kind=kLoop, calls=%fused_computation.160 | loop fusion | flops 1376256 | bytes 7077888 | tf_op jit(solution)/shard_map/reduce_sum | solution.py:73
  148.0 1.4 maximum_divide_fusion
  149.6 96.3 %while.34 = (s32[]{:T(128)}, f32[3,384,512]{2,1,0:T(8,128)S(1)}, s32[3]{0:T(128)S(1)}, s32[3]{0:T(128)S(1)}, s32[]{:T(128)}, /*index=5*/f32[1,256,256]{2,1,0:T(8...) while((s32[]{:T(128)}, f32[3,384,512]{2,1,0:T(8,128)S(1)}, ...), condition=%wide.region_4.5_spmd.clone.clone, body=%wide.region_3.4_spmd.clone.clone.sunk | while | flops 279183360 | bytes 10223899 | solution.py:105
  149.6 1.2 fusion.208
  152.0 1.1 fusion.210
  156.5 2.1 fusion.214
  159.7 3.1 fusion.216
  168.0 1.3 fusion.217
  169.3 13.6 %dynamic_update_slice.42 = f32[3,384,512]{2,1,0:T(8,128)S(1)} dynamic-update-slice(f32[3,384,512]{2,1,0:T(8,128)S(1)} %get-tuple-element.786, f32[3,256,256]{2,1,0:T(8,128)S(1)} %fusion.217, s32[]{:T(128)} %constant.88.clone.1..sunk.1, s32[]{:T(128)S(6)} %select_n.210, s32[]{:T(128)S(6)} %select_n.211) | dynamic-update-slice | bytes 1572868 | tf_op jit(solution)/shard_map/while/body/eval_jaxpr/dynamic_update_slice | solution.py:103
  183.0 1.2 fusion.208
  189.8 2.1 fusion.214
  193.1 3.1 fusion.216
  201.3 1.3 fusion.217
  202.6 11.0 %dynamic_update_slice.42 = f32[3,384,512]{2,1,0:T(8,128)S(1)} dynamic-update-slice(f32[3,384,512]{2,1,0:T(8,128)S(1)} %get-tuple-element.786, f32[3,256,256]{2,1,0:T(8,128)S(1)} %fusion.217, s32[]{:T(128)} %constant.88.clone.1..sunk.1, s32[]{:T(128)S(6)} %select_n.210, s32[]{:T(128)S(6)} %select_n.211) | dynamic-update-slice | bytes 1572868 | tf_op jit(solution)/shard_map/while/body/eval_jaxpr/dynamic_update_slice | solution.py:103
  213.7 1.2 fusion.208
  216.0 1.1 fusion.210
  219.4 1.1 fusion.213
  220.6 2.1 fusion.214
  223.8 3.1 fusion.216
  232.1 1.3 fusion.217
  233.4 12.6 %dynamic_update_slice.42 = f32[3,384,512]{2,1,0:T(8,128)S(1)} dynamic-update-slice(f32[3,384,512]{2,1,0:T(8,128)S(1)} %get-tuple-element.786, f32[3,256,256]{2,1,0:T(8,128)S(1)} %fusion.217, s32[]{:T(128)} %constant.88.clone.1..sunk.1, s32[]{:T(128)S(6)} %select_n.210, s32[]{:T(128)S(6)} %select_n.211) | dynamic-update-slice | bytes 1572868 | tf_op jit(solution)/shard_map/while/body/eval_jaxpr/dynamic_update_slice | solution.py:103
  246.2 1.9 collective-permute-start.2
  248.1 4.0 %collective-permute-start.3 = (f32[3,128,512]{2,1,0:T(8,128)S(1)}, f32[3,128,512]{2,1,0:T(8,128)S(1)}, u32[]{:S(2)}, u32[]{:S(2)}) collective-permute-start(f32[3,128,512]{2,1,0:T(8,128)S(1)} %get-tuple-element.551), channel_id=1, source_target_pairs={{8,0},{16,8},{24,16},{32,24},{40,32},{48,40},{56,48},{64,56},{72,6... | collective-permute-start | bytes 2359304 | tf_op jit(solution)/shard_map/ppermute | solution.py:16
  252.1 15.7 %collective-permute-done.2 = f32[3,128,512]{2,1,0:T(8,128)S(1)} collective-permute-done((f32[3,128,512]{2,1,0:T(8,128)S(1)}, f32[3,128,512]{2,1,0:T(8,128)S(1)}, u32[]{:S(2)}, u32[]{:S(2)}) %collective-permute-start.2) | collective-permute-done | bytes 786464 | tf_op jit(solution)/shard_map/ppermute | solution.py:15
  267.8 3.9 %collective-permute-done.3 = f32[3,128,512]{2,1,0:T(8,128)S(1)} collective-permute-done((f32[3,128,512]{2,1,0:T(8,128)S(1)}, f32[3,128,512]{2,1,0:T(8,128)S(1)}, u32[]{:S(2)}, u32[]{:S(2)}) %collective-permute-start.3) | collective-permute-done | bytes 786464 | tf_op jit(solution)/shard_map/ppermute | solution.py:16
  271.7 1.2 add_add_fusion
  272.9 39.9 %reduce-scatter.2.cloned.1.call-done = f32[3,16,512]{2,1,0:T(8,128)} async-done(((f32[3,128,512]{2,1,0:T(8,128)}), f32[3,16,512]{2,1,0:T(8,128)}) %reduce-scatter.2.cloned.1.call-update) | async-done | bytes 98320 | tf_op jit(solution)/shard_map/reduce_scatter | solution.py:115
  313.5 1.5 fusion.135
  (64 shorter events, 45.7 us)
Async XLA Ops:
  6.5 20.3 %copy-start.1 = (s32[3]{0:T(128)S(1)}, s32[3]{0:T(128)}, u32[]{:S(2)}) copy-start(s32[3]{0:T(128)} %param.13) | copy-start | bytes 40
  6.5 20.3 %copy-start.2 = (s32[3]{0:T(128)S(1)}, s32[3]{0:T(128)}, u32[]{:S(2)}) copy-start(s32[3]{0:T(128)} %param.14) | copy-start | bytes 40
  6.5 138.1 %all-gather.3.cloned.1.call-start = ((), (), s32[]{:S(2)}) async-start(), calls=%async_computation.2 | async-start | bytes 7077888 | tf_op jit(solution)/shard_map/all_gather | solution.py:73
  6.5 15.9 %collective-permute-start = (f32[2,128,512]{2,1,0:T(8,128)}, f32[2,128,512]{2,1,0:T(8,128)S(1)}, u32[]{:S(2)}, u32[]{:S(2)}) collective-permute-start(f32[2,128,512]{2,1,0:T(8,128)} %param.10), channel_id=1, source_target_pairs={{0,8},{8,16},{16,24},{24,32},{32,40},{40,48},{48,56},{56,64},{64,7... | collective-permute-start | bytes 1572872 | tf_op jit(solution)/shard_map/ppermute | solution.py:15
  10.2 15.5 %collective-permute-start.1 = (f32[2,128,512]{2,1,0:T(8,128)}, f32[2,128,512]{2,1,0:T(8,128)S(1)}, u32[]{:S(2)}, u32[]{:S(2)}) collective-permute-start(f32[2,128,512]{2,1,0:T(8,128)} %param.10), channel_id=1, source_target_pairs={{8,0},{16,8},{24,16},{32,24},{40,32},{48,40},{56,48},{64,56},{72,6... | collective-permute-start | bytes 1572872 | tf_op jit(solution)/shard_map/ppermute | solution.py:16
  89.7 223.1 %reduce-scatter.2.cloned.1.call-start = ((), (), s32[]{:S(2)}) async-start(), calls=%async_computation.1 | async-start | bytes 884736 | tf_op jit(solution)/shard_map/reduce_scatter | solution.py:115
  144.6 3.4 %copy-start = (f32[3,256,256]{2,1,0:T(8,128)S(1)}, f32[3,256,256]{2,1,0:T(8,128)}, u32[]{:S(2)}) copy-start(f32[3,256,256]{2,1,0:T(8,128)} %param.12) | copy-start | bytes 2359300
  246.2 21.6 %collective-permute-start.2 = (f32[3,128,512]{2,1,0:T(8,128)S(1)}, f32[3,128,512]{2,1,0:T(8,128)S(1)}, u32[]{:S(2)}, u32[]{:S(2)}) collective-permute-start(f32[3,128,512]{2,1,0:T(8,128)S(1)} %get-tuple-element.550), channel_id=1, source_target_pairs={{0,8},{8,16},{16,24},{24,32},{32,40},{40,48},{48,56},{56,64},{64,7... | collective-permute-start | bytes 2359304 | tf_op jit(solution)/shard_map/ppermute | solution.py:15
  248.1 23.6 %collective-permute-start.3 = (f32[3,128,512]{2,1,0:T(8,128)S(1)}, f32[3,128,512]{2,1,0:T(8,128)S(1)}, u32[]{:S(2)}, u32[]{:S(2)}) collective-permute-start(f32[3,128,512]{2,1,0:T(8,128)S(1)} %get-tuple-element.551), channel_id=1, source_target_pairs={{8,0},{16,8},{24,16},{32,24},{40,32},{48,40},{56,48},{64,56},{72,6... | collective-permute-start | bytes 2359304 | tf_op jit(solution)/shard_map/ppermute | solution.py:16
Sparse Core Ops, SparseCore 0:
  89.9 54.6 all-gather.2
  273.0 39.7 reduce-scatter.1
